TPU v7x, 256 devices: a whole 4x4x8 slice. The times are simulated.
256 devices in a mesh: tok: 32 (over z, x), head: 8 (over y, core).
Axes of the slice: x: 4, y: 4, z: 8, core: 2. Of those that a mesh axis runs over, the one named last changes fastest.
Arguments:
- embeddings: bfloat16 [4096, 4096], P('tok'), may hold values from -6 to 6
- norm_gain: bfloat16 [4096], replicated, may hold values from 0.099609375 to 1.8984375
- query_key_value_weight: bfloat16 [4096, 6144], P(None, 'head'), may hold values from -0.09375 to 0.09375
- embed_table: bfloat16 [65536, 4096], P('tok', 'head'), may hold values from -6 to 6
- rotated_cache_pages: bfloat16 [32, 32, 256, 2048], P('tok', None, None, 'head'), may hold values from -300 to 300
- page_owner_device: int32 [32, 32], P('tok'), may hold values from 0 to 31, each once within a row
- cached_length: int32 [32], P('tok'), may hold values from 2 to 8192, as said below
- vocab_shard: int32 [4096, 1], P('tok'), may hold values from 0 to 31; in each aligned block of 128 rows (0 to 127, 128 to 255, ...) at most 8 rows name the same one
- shard_row: int32 [4096], P('tok'), may hold values from 0 to 2047
- accept: int32 [4096], P('tok'), may hold values from 0 to 1, as said below
Outputs:
- out_first: bfloat16 [4096, 4096], P('tok', 'head')
- out_second: bfloat16 [4096, 4096], P('tok', 'head')
Inputs may be any that keep to these rules, and one draw needn't show every extreme that they name: `page_owner_device`: each row names every device of the tok axis once. `cached_length`: some request has exactly 8192 cached positions. `vocab_shard`: at most 8 of the 128 tokens of one request name the same shard, and some shard is named that often. `accept`: at most 32 accepted tokens in one request's block; some block has exactly 32.
All inputs are finite; a program needn't handle non-finite values.
Results may differ from a plain program's by a relative error of at most 0.017.
The roundings to bfloat16 on the way count: a program that leaves them out, or rounds other values in their place, can miss the bound.
Values may be sent and summed in bfloat16 or wider, within the bound.
No kernel may reach another device: no remote copies, remote signals or barrier semaphores. Data moves between devices by JAX's collectives and lax.ppermute only.
A program may use at most 128 MiB of HBM per device.

v0:
```python
import math
import jax
import jax.numpy as jnp
from jax import lax
from jax.sharding import PartitionSpec as P

QUERY_HEADS = 32
KEY_VALUE_HEADS = 8
HEAD_SIZE = 128
THETA = 500000.0


def angles(positions):
    steps_half = jnp.arange(HEAD_SIZE // 2, dtype=jnp.float32)
    frequency = THETA ** (-(steps_half * 2.0) / HEAD_SIZE)
    return positions.astype(jnp.float32)[:, None] * frequency[None, :]


def rotate(vectors, turning):
    half_width = vectors.shape[-1] // 2
    former = vectors[..., :half_width]
    latter = vectors[..., half_width:]
    cosine = jnp.cos(turning)
    sine_of = jnp.sin(turning)
    return jnp.concatenate(
        [former * cosine - latter * sine_of, latter * cosine + former * sine_of], axis=-1
    )


def project(inputs, norm_gain, query_key_value_weight, positions):
    widened = inputs.astype(jnp.float32)
    inverse = lax.rsqrt(jnp.mean(widened * widened, axis=-1, keepdims=True) + 1e-05)
    normed = (widened * inverse * norm_gain.astype(jnp.float32)).astype(jnp.bfloat16)
    combined = jnp.dot(normed, query_key_value_weight, preferred_element_type=jnp.float32)
    heads_per_group = QUERY_HEADS // KEY_VALUE_HEADS
    combined = combined.reshape(inputs.shape[0], -1, heads_per_group + 2, HEAD_SIZE)
    turning = angles(positions)[:, None, None, :]
    query_vectors = rotate(combined[:, :, :heads_per_group], turning).astype(jnp.bfloat16)
    block_keys = rotate(combined[:, :, heads_per_group : heads_per_group + 1], turning)[
        :, :, 0
    ].astype(jnp.bfloat16)
    block_values = combined[:, :, heads_per_group + 1].astype(jnp.bfloat16)
    return (query_vectors, block_keys, block_values)


def attend(query_vectors, block_keys, block_values, page_keys, page_values, usable):
    factor = 1.0 / math.sqrt(HEAD_SIZE)
    scores_cache = (
        jnp.einsum("bgqd,kgd->gqbk", query_vectors, page_keys, preferred_element_type=jnp.float32)
        * factor
    )
    scores_cache = jnp.where(usable[None, None, None, :], scores_cache, -1e30)
    scores_block = (
        jnp.einsum("bgqd,cgd->gqbc", query_vectors, block_keys, preferred_element_type=jnp.float32)
        * factor
    )
    highest = jnp.maximum(jnp.max(scores_cache, axis=-1), jnp.max(scores_block, axis=-1))[..., None]
    exp_cache = jnp.exp(scores_cache - highest)
    exp_block = jnp.exp(scores_block - highest)
    totals = jnp.sum(exp_cache, axis=-1) + jnp.sum(exp_block, axis=-1)
    weights_cache = exp_cache.astype(jnp.bfloat16)
    weights_block = exp_block.astype(jnp.bfloat16)
    combined = jnp.einsum(
        "gqbk,kgd->bgqd", weights_cache, page_values, preferred_element_type=jnp.float32
    )
    combined = combined + jnp.einsum(
        "gqbc,cgd->bgqd", weights_block, block_values, preferred_element_type=jnp.float32
    )
    result = combined / jnp.transpose(totals, (2, 0, 1))[..., None]
    return result.astype(jnp.bfloat16).reshape(query_vectors.shape[0], -1)


def body(
    embeddings,
    norm_gain,
    query_key_value_weight,
    embed_table,
    rotated_cache_pages,
    page_owner_device,
    cached_length,
    vocab_shard,
    shard_row,
    accept,
):
    members = lax.axis_size("tok")
    length = embeddings.shape[0]
    sources = jnp.arange(members, dtype=jnp.int32)
    positions = cached_length[0] + jnp.arange(length, dtype=jnp.int32)
    query_vectors, block_keys, block_values = project(
        embeddings, norm_gain, query_key_value_weight, positions
    )
    arrived = lax.all_to_all(rotated_cache_pages, "tok", split_axis=1, concat_axis=0, tiled=True)
    page_size = arrived.shape[2]
    arrived = arrived.reshape(members * page_size, -1, 2, HEAD_SIZE)
    page_index = jnp.sum(
        jnp.where(page_owner_device[0][:, None] == sources[None, :], sources[:, None], 0), axis=0
    )
    page_spots = page_index[:, None] * page_size + jnp.arange(page_size, dtype=jnp.int32)[None, :]
    usable = page_spots.reshape(-1) < cached_length[0]
    page_keys = arrived[:, :, 0]
    page_values = arrived[:, :, 1]

    def run_attention(query_rows, key_rows, value_rows):
        return attend(query_rows, key_rows, value_rows, page_keys, page_values, usable)

    output_one = run_attention(query_vectors, block_keys, block_values)
    target_shard = vocab_shard[:, 0]
    capacity = max(2, 2 * length // members)
    chosen = (target_shard[:, None] == sources[None, :]).astype(jnp.int32)
    earlier = (jnp.arange(length)[:, None] > jnp.arange(length)[None, :]).astype(jnp.int32)
    slot_rank = jnp.sum(jnp.dot(earlier, chosen) * chosen, axis=1)
    wanted = jnp.zeros((members, capacity), jnp.int32).at[target_shard, slot_rank].set(shard_row)
    found_rows = jnp.take(
        embed_table, lax.all_to_all(wanted, "tok", split_axis=0, concat_axis=0, tiled=True), axis=0
    )
    returned = lax.all_to_all(found_rows, "tok", split_axis=0, concat_axis=0, tiled=True)
    replacement = returned[target_shard, slot_rank]
    full_rows = lax.all_gather(replacement, "head", axis=1, tiled=True)
    replaced = jnp.where(accept[:, None] == 1, full_rows, embeddings)
    queries_two, keys_two, values_two = project(
        replaced, norm_gain, query_key_value_weight, positions
    )
    output_two = run_attention(queries_two, keys_two, values_two)
    return (output_one, output_two)


def solution(mesh):
    return jax.shard_map(
        body,
        mesh=mesh,
        in_specs=(
            P("tok", None),
            P(),
            P(None, "head"),
            P("tok", "head"),
            P("tok", None, None, "head"),
            P("tok", None),
            P("tok"),
            P("tok", None),
            P("tok"),
            P("tok"),
        ),
        out_specs=(P("tok", "head"), P("tok", "head")),
        check_vma=False,
    )
```

profile of v0, /device:TPU:12, one launch (start us, length us, event | category | flops | bytes accessed | tf_op | source)
XLA Modules:
  0.0 241.9 jit_solution(14365437352633551345)
XLA Ops:
  7.2 1.0 fusion.36
  8.8 10.9 %scatter_fusion = s32[32,8]{0,1:T(8,128)S(1)} fusion(s32[32,8]{0,1:T(8,128)S(1)} %broadcast_in_dim.55, s32[128]{0:T(128)S(1)} %get-tuple-element.14, s32[128]{0:T(128)} %param.18), kind=kCustom, calls=%fused_computation.2 | custom fusion | bytes 2560 | tf_op jit(solution)/shard_map/scatter | solution.py:112
  19.9 19.1 %all_to_all.29 = s32[32,1,8]{2,1,0:T(1,128)S(1)} all-to-all(s32[32,1,8]{2,1,0:T(1,128)S(1)} %copy.91), channel_id=1, replica_groups=mesh['tok'=32,'head'=8] {'tok'}, dimensions={0} | all-to-all | bytes 2048 | tf_op jit(solution)/shard_map/all_to_all | solution.py:114
  39.3 1.2 gather_fusion
  40.5 15.1 %all_to_all.30 = bf16[32,8,512]{2,1,0:T(8,128)(2,1)S(1)} all-to-all(bf16[32,8,512]{2,1,0:T(8,128)(2,1)S(1)} %bitcast_select_fusion.2), channel_id=1, replica_groups=mesh['tok'=32,'head'=8] {'tok'}, dimensions={0} | all-to-all | bytes 524288 | tf_op jit(solution)/shard_map/all_to_all | solution.py:116
  55.6 6.6 %all-to-all-start = ((bf16[1,32,256,256]{3,2,0,1:T(8,128)(2,1)}), bf16[1,32,256,256]{3,2,0,1:T(8,128)(2,1)}, u32[]{:S(2)}, u32[]{:S(2)}) async-start(bf16[1,32,256,256]{3,2,0,1:T(8,128)(2,1)} %bitcast.163), calls=%async_computation | async-start | bytes 8388608 | tf_op jit(solution)/shard_map/all_to_all | solution.py:92
  62.3 1.9 gather_fusion.1
  65.5 25.3 %all-gather.2.cloned.1.call-done = bf16[128,4096]{1,0:T(8,128)(2,1)} async-done(((bf16[128,512]{1,0:T(8,128)(2,1)}), bf16[128,4096]{1,0:T(8,128)(2,1)}) %all-gather.2.cloned.1.call-update) | async-done | bytes 1048592 | tf_op jit(solution)/shard_map/all_gather | solution.py:118
  90.8 1.9 fusion.17
  92.7 5.8 %fusion.41 = f32[128,768]{0,1:T(8,128)S(1)} fusion(bf16[4096,768]{1,0:T(8,128)(2,1)} %param.12, f32[128]{0:T(128)S(1)} %get-tuple-element.44, f32[4096]{0:T(1024)S(1)} %convert_element_type.83, bf16[128,4096]{1,0:T(8,128)(2,1)} %all-gather.2.cloned.1.call-done, bf16[128,4096]{1,0:T(8,128)(2,1)S(1)} %copy-done.3, pred[128]{0:T(512)(128)(4,1)S(1)} %broadcast_compare_fusion), kind=kOutput, calls=%fused_computation.48 | convolution fusion | flops 807927808 | bytes 8798848 | tf_op jit(solution)/shard_map/dot_general | solution.py:34
  98.8 5.4 %fusion.43 = f32[128,768]{0,1:T(8,128)S(1)} fusion(bf16[4096,768]{1,0:T(8,128)(2,1)} %param.12, bf16[128,4096]{1,0:T(8,128)(2,1)S(1)} %copy-done.3, f32[4096]{0:T(1024)S(1)} %convert_element_type.83, f32[128]{0:T(128)S(1)} %get-tuple-element.45), kind=kOutput, calls=%fused_computation.49 | convolution fusion | flops 807403520 | bytes 7750144 | tf_op jit(solution)/shard_map/dot_general | solution.py:34
  105.5 49.8 %all-to-all-done = bf16[1,32,256,256]{3,2,0,1:T(8,128)(2,1)} async-done(((bf16[1,32,256,256]{3,2,0,1:T(8,128)(2,1)}), bf16[1,32,256,256]{3,2,0,1:T(8,128)(2,1)}, u32[]{:S(2)}, u32[]{:S(2)}) %all-to-all-start) | async-done | bytes 4194336 | tf_op jit(solution)/shard_map/all_to_all | solution.py:92
  155.3 6.9 %reshape.435 = bf16[8192,1,2,128]{3,2,0,1:T(2,128)(2,1)} reshape(bf16[1,32,256,256]{3,2,0,1:T(8,128)(2,1)} %all-to-all-done) | data formatting | bytes 8388608 | tf_op jit(solution)/shard_map/reshape | solution.py:94
  162.3 9.8 %fusion.95 = (bf16[8192,1,1,128]{3,2,0,1:T(2,128)(2,1)S(1)}, bf16[8192,1,1,128]{3,2,0,1:T(2,128)(2,1)}) fusion(bf16[8192,1,2,128]{3,2,0,1:T(2,128)(2,1)} %reshape.435), kind=kLoop, calls=%fused_computation.135 | loop fusion | bytes 8388608 | tf_op jit(solution)/shard_map/slice | solution.py:100
  172.1 8.3 %fusion.98 = (f32[4,128]{1,0:T(4,128)}, f32[1,4,128,8192]{3,2,1,0:T(8,128)}) fusion(bf16[8192,1,1,128]{3,2,0,1:T(2,128)(2,1)S(1)} %get-tuple-element.16, bf16[128,4,64]{2,0,1:T(8,128)(2,1)S(1)} %get-tuple-element.30, bf16[128,4,64]{2,0,1:T(8,128)(2,1)S(1)} %get-tuple-element.31, pred[8192]{0:T(1024)(128)(4,1)S(1)} %lt.48), kind=kOutput, calls=%fused_computation.138 | convolution fusion | flops 1086586368 | bytes 19015680 | tf_op jit(solution)/shard_map/bgqd,kgd->gqbk/dot_general | solution.py:49
  180.3 7.7 %fusion.100 = (f32[4,128]{1,0:T(4,128)S(1)}, f32[1,4,128,8192]{3,2,1,0:T(8,128)}) fusion(bf16[8192,1,1,128]{3,2,0,1:T(2,128)(2,1)S(1)} %get-tuple-element.16, bf16[128,4,64]{2,0,1:T(8,128)(2,1)S(1)} %get-tuple-element.19, bf16[128,4,64]{2,0,1:T(8,128)(2,1)S(1)} %get-tuple-element.18, pred[8192]{0:T(1024)(128)(4,1)S(1)} %lt.48), kind=kOutput, calls=%fused_computation.140 | convolution fusion | flops 1086586368 | bytes 19015680 | tf_op jit(solution)/shard_map/bgqd,kgd->gqbk/dot_general | solution.py:49
  188.0 8.3 %copy.114 = bf16[8192,1,1,128]{0,3,2,1:T(8,128)(2,1)S(1)} copy(bf16[8192,1,1,128]{3,2,0,1:T(2,128)(2,1)} %get-tuple-element.17) | data formatting | bytes 4194304
  196.4 8.9 %fusion.2 = f32[4,128]{1,0:T(4,128)S(1)} fusion(f32[1,4,128,8192]{3,2,1,0:T(8,128)} %get-tuple-element.37, f32[4,128]{1,0:T(4,128)S(1)} %max.18), kind=kLoop, calls=%fused_computation.9 | loop fusion | flops 8388096 | bytes 16781312 | tf_op jit(solution)/shard_map/reduce_sum | solution.py:60
  205.2 8.8 %fusion.26 = f32[128,4,128]{2,0,1:T(8,128)S(1)} fusion(bf16[8192,1,1,128]{0,3,2,1:T(8,128)(2,1)S(1)} %copy.114, f32[1,4,128,8192]{3,2,1,0:T(8,128)} %get-tuple-element.37, f32[4,128]{1,0:T(4,128)S(1)} %max.18), kind=kOutput, calls=%fused_computation.40 | convolution fusion | flops 1082130432 | bytes 19138560 | tf_op jit(solution)/shard_map/gqbk,kgd->bgqd/dot_general | solution.py:63
  214.0 8.4 %fusion.31 = f32[128,4,128]{2,0,1:T(8,128)S(1)} fusion(bf16[8192,1,1,128]{0,3,2,1:T(8,128)(2,1)} %copy-done.2, f32[1,4,128,8192]{3,2,1,0:T(8,128)} %get-tuple-element.41, f32[4,128]{1,0:T(4,128)S(1)} %max.19), kind=kOutput, calls=%fused_computation.41 | convolution fusion | flops 1082130432 | bytes 19138560 | tf_op jit(solution)/shard_map/gqbk,kgd->bgqd/dot_general | solution.py:63
  222.4 8.1 %fusion.4 = f32[4,128]{1,0:T(4,128)S(1)} fusion(f32[1,4,128,8192]{3,2,1,0:T(8,128)} %get-tuple-element.41, f32[4,128]{1,0:T(4,128)S(1)} %max.19), kind=kLoop, calls=%fused_computation.11 | loop fusion | flops 8388096 | bytes 16781312 | tf_op jit(solution)/shard_map/reduce_sum | solution.py:60
  230.6 0.9 fusion.38
  231.5 1.7 copy.99
  233.2 1.0 fusion.40
  (57 shorter events, 4.1 us)
Async XLA Ops:
  7.2 32.0 %copy-start = (bf16[2048,512]{1,0:T(8,128)(2,1)S(1)}, bf16[2048,512]{1,0:T(8,128)(2,1)}, u32[]{:S(2)}) copy-start(bf16[2048,512]{1,0:T(8,128)(2,1)} %param.13) | copy-start | bytes 6291460
  39.2 25.1 %copy-start.6 = (bf16[4096]{0:T(1024)(128)(2,1)S(1)}, bf16[4096]{0:T(1024)(128)(2,1)}, u32[]{:S(2)}) copy-start(bf16[4096]{0:T(1024)(128)(2,1)} %param.11) | copy-start | bytes 24580
  39.2 25.7 %copy-start.7 = (s32[1,32]{1,0:T(1,128)S(1)}, s32[1,32]{1,0:T(1,128)}, u32[]{:S(2)}) copy-start(s32[1,32]{1,0:T(1,128)} %param.15) | copy-start | bytes 388
  39.2 25.9 %copy-start.8 = (s32[128]{0:T(128)S(1)}, s32[128]{0:T(128)}, u32[]{:S(2)}) copy-start(s32[128]{0:T(128)} %param.19) | copy-start | bytes 1540
  39.2 51.6 %copy-start.3 = (bf16[128,4096]{1,0:T(8,128)(2,1)S(1)}, bf16[128,4096]{1,0:T(8,128)(2,1)}, u32[]{:S(2)}) copy-start(bf16[128,4096]{1,0:T(8,128)(2,1)} %param.10) | copy-start | bytes 3145732
  55.6 99.7 %all-to-all-start = ((bf16[1,32,256,256]{3,2,0,1:T(8,128)(2,1)}), bf16[1,32,256,256]{3,2,0,1:T(8,128)(2,1)}, u32[]{:S(2)}, u32[]{:S(2)}) async-start(bf16[1,32,256,256]{3,2,0,1:T(8,128)(2,1)} %bitcast.163), calls=%async_computation | async-start | bytes 8388608 | tf_op jit(solution)/shard_map/all_to_all | solution.py:92
  62.2 28.6 %all-gather.2.cloned.1.call-start = ((), (), s32[]{:S(2)}) async-start(), calls=%async_computation.3 | async-start | bytes 1179648 | tf_op jit(solution)/shard_map/all_gather | solution.py:118
  98.5 6.7 %copy-start.4 = (f32[128,768]{0,1:T(8,128)}, f32[128,768]{0,1:T(8,128)S(1)}, u32[]{:S(2)}) copy-start(f32[128,768]{0,1:T(8,128)S(1)} %fusion.41) | copy-start | bytes 1179652
  188.0 8.4 %copy-start.5 = (f32[4,128]{1,0:T(4,128)S(1)}, f32[4,128]{1,0:T(4,128)}, u32[]{:S(2)}) copy-start(f32[4,128]{1,0:T(4,128)} %get-tuple-element.36) | copy-start | bytes 6148
  196.4 8.9 %copy-start.2 = (bf16[8192,1,1,128]{0,3,2,1:T(8,128)(2,1)}, bf16[8192,1,1,128]{0,3,2,1:T(8,128)(2,1)S(1)}, u32[]{:S(2)}) copy-start(bf16[8192,1,1,128]{0,3,2,1:T(8,128)(2,1)S(1)} %copy.114) | copy-start | bytes 6291460
  214.0 21.0 %copy-start.1 = (bf16[2048,512]{1,0:T(8,128)(2,1)S(1)}, bf16[2048,512]{1,0:T(8,128)(2,1)}, u32[]{:S(2)}) copy-start(bf16[2048,512]{1,0:T(8,128)(2,1)} %param.13) | copy-start | bytes 6291460
Sparse Core Ops, SparseCore 0:
  65.5 25.3 all-gather.1
where the time goes:
time: 243 us; the launch traced here: 242 us
  waiting for transfers between devices  75.2 us (31%)
  matrix products  47.7 us (20%)
  local copies, waits for them, and re-layouts  42.5 us (17%)
  blocking collectives  34.2 us (14%)
  other arithmetic  20.6 us (8%)
  between operations  15 us (6%)
  starting transfers between devices  6.66 us (3%)
    all_to_all x1, waiting for transfers between devices, body(): lax.all_to_all(rotated_cache_pages, 'tok', split_axis=1, concat_axis=0, t...  49.8 us
    all_gather x1, waiting for transfers between devices, body(): full_rows = lax.all_gather(replacement, 'head', axis=1, tiled=True)  25.3 us
    all_to_all x1, blocking collectives, body(): lax.all_to_all(wanted, 'tok', split_axis=0, concat_axis=0, tiled=True)  19.1 us
    dot_general x2, matrix products, attend(): jnp.einsum('gqbk,kgd->bgqd', weights_cache, page_values, preferred_elemen...  17.1 us
    reduce_sum x4, other arithmetic, attend(): totals = jnp.sum(exp_cache, axis=-1) + jnp.sum(exp_block, axis=-1)  17.1 us
    dot_general x2, matrix products, attend(): jnp.einsum('bgqd,kgd->gqbk', query_vectors, page_keys, preferred_element_...  15.9 us
    all_to_all x1, blocking collectives, body(): lax.all_to_all(found_rows, 'tok', split_axis=0, concat_axis=0, tiled=True)  15.1 us
    unnamed x25, local copies, waits for them, and re-layouts  11.3 us
  transfers between devices with their start and end apart: 2, of which 2 were waited for; matrix products, arithmetic and copies ran while one was open for 7% of the time, Pallas kernels for 0%

commit v1 on v0

--- a/solution.py
+++ b/solution.py
@@ -89,7 +89,15 @@
     query_vectors, block_keys, block_values = project(
         embeddings, norm_gain, query_key_value_weight, positions
     )
-    arrived = lax.all_to_all(rotated_cache_pages, "tok", split_axis=1, concat_axis=0, tiled=True)
+    arrived = jnp.concatenate(
+        lax.all_to_all(
+            jnp.stack(jnp.split(rotated_cache_pages, lax.axis_size("tok"), axis=1), axis=0),
+            concat_axis=0,
+            split_axis=0,
+            axis_name="tok",
+        ),
+        axis=0,
+    )
     page_size = arrived.shape[2]
     arrived = arrived.reshape(members * page_size, -1, 2, HEAD_SIZE)
     page_index = jnp.sum(

time: 243 us -> 275 us (1.13)
  local copies, waits for them, and re-layouts: 42.5 us -> 92.1 us
  blocking collectives: 34.2 us -> 0 us
  starting transfers between devices: 6.66 us -> 27.8 us
  matrix products: 47.7 us -> 40.4 us
  waiting for transfers between devices: 75.2 us -> 80.6 us
  other arithmetic: 20.6 us -> 15.7 us
    unnamed x25 -> x58, local copies, waits for them, and re-layouts: 11.3 us -> 58.8 us
    all_to_all x2 -> x0, blocking collectives: 34.2 us -> none  [the longest x1 19.1 us: body(): lax.all_to_all(wanted, 'tok', split_axis=0, concat_axis=0, tiled=True)]
    all_to_all x1 -> x3, starting transfers between devices: 6.62 us -> 27.7 us  [the longest x1 11.6 us: body(): lax.all_to_all(wanted, 'tok', split_axis=0, concat_axis=0, tiled=True)]
    another operation x0 -> x2, local copies, waits for them, and re-layouts: none -> 8.5 us  [the longest x1 6.92 us: body(): arrived = arrived.reshape(members * page_size, -1, 2, HEAD_SIZE)]
    reshape x1 -> x0, local copies, waits for them, and re-layouts: 6.92 us -> none  [body(): arrived = arrived.reshape(members * page_size, -1, 2, HEAD_SIZE)]
    reduce_sum x4 -> x3, other arithmetic: 17.1 us -> 11.5 us  [attend(): totals = jnp.sum(exp_cache, axis=-1) + jnp.sum(exp_block, axis=-1)]
    dot_general x2, matrix products: 17.1 us -> 11.8 us  [attend(): jnp.einsum('gqbk,kgd->bgqd', weights_cache, page_values, preferred_elemen...]
    all_to_all x1 -> x3, waiting for transfers between devices: 49.8 us -> 55.2 us  [the longest x1 49.2 us: body(): lax.all_to_all(jnp.stack(jnp.split(rotated_cache_pages, lax.axis_size('to...]
  transfers between devices with their start and end apart: 2 -> 4, of which waited for: 2 -> 3; matrix products, arithmetic and copies ran while one was open for 7% -> 25% of each run, Pallas kernels for 0% -> 0%
where the time goes in v1:
time: 275 us; the launch traced here: 272 us
  local copies, waits for them, and re-layouts  92.1 us (33%)
  waiting for transfers between devices  80.6 us (29%)
  matrix products  40.4 us (15%)
  starting transfers between devices  27.8 us (10%)
  other arithmetic  15.7 us (6%)
  between operations  15 us (5%)
    unnamed x58, local copies, waits for them, and re-layouts  58.8 us
    all_to_all x1, waiting for transfers between devices, body(): lax.all_to_all(jnp.stack(jnp.split(rotated_cache_pages, lax.axis_size('to...  49.2 us
    all_gather x1, waiting for transfers between devices, body(): full_rows = lax.all_gather(replacement, 'head', axis=1, tiled=True)  25.4 us
    dot_general x2, matrix products, attend(): jnp.einsum('bgqd,kgd->gqbk', query_vectors, page_keys, preferred_element_...  14.7 us
    dot_general x2, matrix products, attend(): jnp.einsum('gqbk,kgd->bgqd', weights_cache, page_values, preferred_elemen...  11.8 us
    all_to_all x1, starting transfers between devices, body(): lax.all_to_all(wanted, 'tok', split_axis=0, concat_axis=0, tiled=True)  11.6 us
    reduce_sum x3, other arithmetic, attend(): totals = jnp.sum(exp_cache, axis=-1) + jnp.sum(exp_block, axis=-1)  11.5 us
    dot_general x2, matrix products, project(): jnp.dot(normed, query_key_value_weight, preferred_element_type=jnp.float32)  11.1 us
  transfers between devices with their start and end apart: 4, of which 3 were waited for; matrix products, arithmetic and copies ran while one was open for 25% of the time, Pallas kernels for 0%

profile of v1, /device:TPU:12, one launch (start us, length us, event | category | flops | bytes accessed | tf_op | source)
XLA Modules:
  0.0 271.6 jit_solution(3139468339772748646)
XLA Ops:
  8.8 10.9 %scatter_fusion = s32[32,8]{0,1:T(8,128)S(1)} fusion(s32[32,8]{0,1:T(8,128)S(1)} %broadcast_in_dim.55, s32[128]{0:T(128)S(1)} %get-tuple-element.18, s32[128]{0:T(128)} %param.18), kind=kCustom, calls=%fused_computation.2 | custom fusion | bytes 2560 | tf_op jit(solution)/shard_map/scatter | solution.py:120
  20.5 11.6 %all-to-all-start.1 = ((s32[32,1,8]{2,1,0:T(1,128)}), s32[32,1,8]{2,1,0:T(1,128)S(1)}, u32[]{:S(2)}, u32[]{:S(2)}) async-start(s32[32,1,8]{2,1,0:T(1,128)} %copy.97), calls=%async_computation.1 | async-start | bytes 32768 | tf_op jit(solution)/shard_map/all_to_all | solution.py:122
  36.7 1.6 bitcast_dynamic-update-slice_fusion.28
  47.7 1.6 bitcast_dynamic-update-slice_fusion.21
  53.9 1.6 bitcast_dynamic-update-slice_fusion.17
  68.0 1.6 bitcast_dynamic-update-slice_fusion.8
  79.6 9.8 %all-to-all-start.2 = ((bf16[32,8,512]{2,1,0:T(8,128)(2,1)}), bf16[32,8,512]{2,1,0:T(8,128)(2,1)S(1)}, u32[]{:S(2)}, u32[]{:S(2)}) async-start(bf16[32,8,512]{2,1,0:T(8,128)(2,1)} %bitcast_select_fusion.2), calls=%async_computation.2 | async-start | bytes 524288 | tf_op jit(solution)/shard_map/all_to_all | solution.py:124
  92.5 1.6 bitcast_dynamic-update-slice_fusion
  94.1 5.9 %all-to-all-done.2 = bf16[32,8,512]{2,1,0:T(8,128)(2,1)S(1)} async-done(((bf16[32,8,512]{2,1,0:T(8,128)(2,1)}), bf16[32,8,512]{2,1,0:T(8,128)(2,1)S(1)}, u32[]{:S(2)}, u32[]{:S(2)}) %all-to-all-start.2) | async-done | bytes 262176 | tf_op jit(solution)/shard_map/all_to_all | solution.py:124
  100.0 6.4 %all-to-all-start = ((bf16[32,1,1,256,256]{4,3,2,1,0:T(8,128)(2,1)}), bf16[32,1,1,256,256]{4,3,2,1,0:T(8,128)(2,1)}, u32[]{:S(2)}, u32[]{:S(2)}) async-start(bf16[32,1,1,256,256]{4,3,2,1,0:T(8,128)(2,1)} %bitcast_dynamic-update-slice_fusion), calls=%async_computation | async-start | bytes 8388608 | tf_op jit(solution)/shard_map/all_to_all | solution.py:93
  106.4 1.9 gather_fusion.1
  109.6 25.4 %all-gather.2.cloned.1.call-done = bf16[128,4096]{1,0:T(8,128)(2,1)} async-done(((bf16[128,512]{1,0:T(8,128)(2,1)}), bf16[128,4096]{1,0:T(8,128)(2,1)}) %all-gather.2.cloned.1.call-update) | async-done | bytes 1048592 | tf_op jit(solution)/shard_map/all_gather | solution.py:126
  135.0 1.9 fusion.17
  136.9 5.7 %fusion.31 = f32[128,768]{0,1:T(8,128)S(1)} fusion(bf16[4096,768]{1,0:T(8,128)(2,1)} %param.12, f32[128]{0:T(128)S(1)} %get-tuple-element.45, f32[4096]{0:T(1024)S(1)} %convert_element_type.83, bf16[128,4096]{1,0:T(8,128)(2,1)} %all-gather.2.cloned.1.call-done, bf16[128,4096]{1,0:T(8,128)(2,1)S(1)} %copy-done.3, pred[128]{0:T(512)(128)(4,1)S(1)} %broadcast_compare_fusion), kind=kOutput, calls=%fused_computation.48 | convolution fusion | flops 807927808 | bytes 8798848 | tf_op jit(solution)/shard_map/dot_general | solution.py:34
  143.0 5.4 %fusion.33 = f32[128,768]{0,1:T(8,128)S(1)} fusion(bf16[4096,768]{1,0:T(8,128)(2,1)} %param.12, bf16[128,4096]{1,0:T(8,128)(2,1)S(1)} %copy-done.3, f32[4096]{0:T(1024)S(1)} %convert_element_type.83, f32[128]{0:T(128)S(1)} %get-tuple-element.46), kind=kOutput, calls=%fused_computation.49 | convolution fusion | flops 807403520 | bytes 7750144 | tf_op jit(solution)/shard_map/dot_general | solution.py:34
  149.6 49.2 %all-to-all-done = bf16[32,1,1,256,256]{4,3,2,1,0:T(8,128)(2,1)} async-done(((bf16[32,1,1,256,256]{4,3,2,1,0:T(8,128)(2,1)}), bf16[32,1,1,256,256]{4,3,2,1,0:T(8,128)(2,1)}, u32[]{:S(2)}, u32[]{:S(2)}) %all-to-all-start) | async-done | bytes 4194336 | tf_op jit(solution)/shard_map/all_to_all | solution.py:93
  198.8 6.9 %reshape.423 = bf16[8192,1,2,128]{3,2,0,1:T(2,128)(2,1)} reshape(bf16[32,1,1,256,256]{4,3,2,1,0:T(8,128)(2,1)} %all-to-all-done) | data formatting | bytes 8388608 | tf_op jit(solution)/shard_map/reshape;reshape | solution.py:102
  205.7 9.8 %fusion.91 = (bf16[8192,1,1,128]{3,2,0,1:T(2,128)(2,1)}, bf16[8192,1,1,128]{3,2,0,1:T(2,128)(2,1)}) fusion(bf16[8192,1,2,128]{3,2,0,1:T(2,128)(2,1)} %reshape.423), kind=kLoop, calls=%fused_computation.173 | loop fusion | bytes 8388608 | tf_op jit(solution)/shard_map/slice | solution.py:109
  215.5 8.3 %copy.120 = bf16[8192,1,1,128]{0,3,2,1:T(8,128)(2,1)S(1)} copy(bf16[8192,1,1,128]{3,2,0,1:T(2,128)(2,1)} %get-tuple-element.20) | data formatting | bytes 4194304
  223.9 5.4 %fusion.40 = f32[8192,128,4]{1,0,2:T(8,128)S(1)} fusion(bf16[8192,1,1,128]{3,2,0,1:T(2,128)(2,1)} %get-tuple-element.21, bf16[128,4,64]{2,0,1:T(8,128)(2,1)S(1)} %get-tuple-element.34, bf16[128,4,64]{2,0,1:T(8,128)(2,1)S(1)} %get-tuple-element.35), kind=kOutput, calls=%fused_computation.56 | convolution fusion | flops 1074003968 | bytes 19005440 | tf_op jit(solution)/shard_map/bgqd,kgd->gqbk/dot_general | solution.py:49
  229.3 9.3 %bitcast_reduce_fusion = (f32[4,128]{1,0:T(4,128)S(1)}, f32[4,128]{1,0:T(4,128)S(1)}, f32[8192,128,4]{1,0,2:T(8,128)}) fusion(pred[8192]{0:T(1024)(128)(4,1)S(1)} %lt.48, f32[8192,128,4]{1,0,2:T(8,128)S(1)} %fusion.40, bf16[128,4,64]{2,0,1:T(8,128)(2,1)S(1)} %get-tuple-element.23, bf16[128,4,64]{2,0,1:T(8,128)(2,1)S(1)} %get-tuple-element.22, ...), kind=kOutput, calls=%fused_computation.4 | convolution fusion | flops 1099168768 | bytes 35794944 | tf_op jit(solution)/shard_map/bgqd,kgd->gqbk/dot_general | solution.py:49
  238.6 3.6 %fusion.8 = f32[128,4,128]{2,0,1:T(8,128)S(1)} fusion(f32[8192,128,4]{1,0,2:T(8,128)S(1)} %fusion.40, f32[4,128]{1,0:T(4,128)S(1)} %max.18, pred[8192]{0:T(1024)(128)(4,1)S(1)} %lt.48, bf16[8192,1,1,128]{0,3,2,1:T(8,128)(2,1)S(1)} %copy.120), kind=kOutput, calls=%fused_computation.17 | convolution fusion | flops 1090519040 | bytes 19146752 | tf_op jit(solution)/shard_map/gqbk,kgd->bgqd/dot_general | solution.py:63
  242.2 11.4 %fusion.4 = (f32[4,128]{1,0:T(4,128)S(1)}, f32[4,128]{1,0:T(4,128)S(1)}) fusion(f32[8192,128,4]{1,0,2:T(8,128)} %get-tuple-element.40, f32[4,128]{1,0:T(4,128)S(1)} %max.19, pred[8192]{0:T(1024)(128)(4,1)S(1)} %lt.48, f32[4,128]{1,0:T(4,128)S(1)} %max.18, f32[8192,128,4]{1,0,2:T(8,128)S(1)} %fusion.40), kind=kLoop, calls=%fused_computation.13 | loop fusion | flops 33553408 | bytes 33570816 | tf_op jit(solution)/shard_map/reduce_sum | solution.py:60
  253.6 8.2 %fusion.10 = f32[128,4,128]{2,0,1:T(8,128)S(1)} fusion(f32[8192,128,4]{1,0,2:T(8,128)} %get-tuple-element.40, f32[4,128]{1,0:T(4,128)S(1)} %max.19, pred[8192]{0:T(1024)(128)(4,1)S(1)} %lt.48, bf16[8192,1,1,128]{0,3,2,1:T(8,128)(2,1)S(1)} %copy-done.5), kind=kOutput, calls=%fused_computation.18 | convolution fusion | flops 1090519040 | bytes 19146752 | tf_op jit(solution)/shard_map/gqbk,kgd->bgqd/dot_general | solution.py:63
  (92 shorter events, 51.7 us)
Async XLA Ops:
  7.2 70.5 %copy-start = (bf16[2048,512]{1,0:T(8,128)(2,1)S(1)}, bf16[2048,512]{1,0:T(8,128)(2,1)}, u32[]{:S(2)}) copy-start(bf16[2048,512]{1,0:T(8,128)(2,1)} %param.13) | copy-start | bytes 6291460
  20.5 56.9 %all-to-all-start.1 = ((s32[32,1,8]{2,1,0:T(1,128)}), s32[32,1,8]{2,1,0:T(1,128)S(1)}, u32[]{:S(2)}, u32[]{:S(2)}) async-start(s32[32,1,8]{2,1,0:T(1,128)} %copy.97), calls=%async_computation.1 | async-start | bytes 32768 | tf_op jit(solution)/shard_map/all_to_all | solution.py:122
  79.6 20.4 %all-to-all-start.2 = ((bf16[32,8,512]{2,1,0:T(8,128)(2,1)}), bf16[32,8,512]{2,1,0:T(8,128)(2,1)S(1)}, u32[]{:S(2)}, u32[]{:S(2)}) async-start(bf16[32,8,512]{2,1,0:T(8,128)(2,1)} %bitcast_select_fusion.2), calls=%async_computation.2 | async-start | bytes 524288 | tf_op jit(solution)/shard_map/all_to_all | solution.py:124
  94.1 15.0 %copy-start.8 = (s32[1,32]{1,0:T(1,128)S(1)}, s32[1,32]{1,0:T(1,128)}, u32[]{:S(2)}) copy-start(s32[1,32]{1,0:T(1,128)} %param.15) | copy-start | bytes 388
  94.1 15.2 %copy-start.7 = (bf16[4096]{0:T(1024)(128)(2,1)S(1)}, bf16[4096]{0:T(1024)(128)(2,1)}, u32[]{:S(2)}) copy-start(bf16[4096]{0:T(1024)(128)(2,1)} %param.11) | copy-start | bytes 24580
  94.1 15.2 %copy-start.9 = (s32[128]{0:T(128)S(1)}, s32[128]{0:T(128)}, u32[]{:S(2)}) copy-start(s32[128]{0:T(128)} %param.19) | copy-start | bytes 1540
  94.1 41.0 %copy-start.3 = (bf16[128,4096]{1,0:T(8,128)(2,1)S(1)}, bf16[128,4096]{1,0:T(8,128)(2,1)}, u32[]{:S(2)}) copy-start(bf16[128,4096]{1,0:T(8,128)(2,1)} %param.10) | copy-start | bytes 3145732
  100.0 98.8 %all-to-all-start = ((bf16[32,1,1,256,256]{4,3,2,1,0:T(8,128)(2,1)}), bf16[32,1,1,256,256]{4,3,2,1,0:T(8,128)(2,1)}, u32[]{:S(2)}, u32[]{:S(2)}) async-start(bf16[32,1,1,256,256]{4,3,2,1,0:T(8,128)(2,1)} %bitcast_dynamic-update-slice_fusion), calls=%async_computation | async-start | bytes 8388608 | tf_op jit(solution)/shard_map/all_to_all | solution.py:93
  106.4 28.7 %all-gather.2.cloned.1.call-start = ((), (), s32[]{:S(2)}) async-start(), calls=%async_computation.3 | async-start | bytes 1179648 | tf_op jit(solution)/shard_map/all_gather | solution.py:126
  142.7 6.0 %copy-start.6 = (f32[128,768]{0,1:T(8,128)}, f32[128,768]{0,1:T(8,128)S(1)}, u32[]{:S(2)}) copy-start(f32[128,768]{0,1:T(8,128)S(1)} %fusion.31) | copy-start | bytes 1179652
  223.9 14.7 %copy-start.4 = (bf16[8192,1,1,128]{0,3,2,1:T(8,128)(2,1)}, bf16[8192,1,1,128]{0,3,2,1:T(8,128)(2,1)S(1)}, u32[]{:S(2)}) copy-start(bf16[8192,1,1,128]{0,3,2,1:T(8,128)(2,1)S(1)} %copy.120) | copy-start | bytes 6291460
  223.9 5.4 %copy-start.2 = (bf16[8192,1,1,128]{3,2,0,1:T(2,128)(2,1)S(1)}, bf16[8192,1,1,128]{3,2,0,1:T(2,128)(2,1)}, u32[]{:S(2)}) copy-start(bf16[8192,1,1,128]{3,2,0,1:T(2,128)(2,1)} %get-tuple-element.21) | copy-start | bytes 6291460
  242.2 11.4 %copy-start.5 = (bf16[8192,1,1,128]{0,3,2,1:T(8,128)(2,1)S(1)}, bf16[8192,1,1,128]{0,3,2,1:T(8,128)(2,1)}, u32[]{:S(2)}) copy-start(bf16[8192,1,1,128]{0,3,2,1:T(8,128)(2,1)} %copy-done.4) | copy-start | bytes 6291460
  253.6 11.2 %copy-start.1 = (bf16[2048,512]{1,0:T(8,128)(2,1)S(1)}, bf16[2048,512]{1,0:T(8,128)(2,1)}, u32[]{:S(2)}) copy-start(bf16[2048,512]{1,0:T(8,128)(2,1)} %param.13) | copy-start | bytes 6291460
Sparse Core Ops, SparseCore 0:
  109.6 25.3 all-gather.1
